TPU v7x, 32 devices: a whole 2x2x4 slice. The times are simulated.
32 devices in a mesh: groups: 2 (over y), events: 8 (over z, x), heads: 2 (over core).
Axes of the slice: x: 2, y: 2, z: 4, core: 2. Of those that a mesh axis runs over, the one named last changes fastest.
Arguments:
- inputs: bfloat16 [256, 1024], P(('groups', 'events')), parts along dimension 0, may hold values from -6 to 6
- cand_user: int32 [256], P('groups'), parts along dimension 0, may hold values from 0 to 3, as said below
- event_user: int32 [8192], P(('groups', 'events')), parts along dimension 0, may hold values from 0 to 3, as said below
- event_count: int32 [16], P(('groups', 'events')), parts along dimension 0, may hold values from 128 to 512, as said below
- w_qu: bfloat16 [1024, 2, 1024], P(None, None, 'heads'), may hold values from -0.1875 to 0.1875
- keys: bfloat16 [8192, 1024], P(('groups', 'events'), 'heads'), parts along dimension 0, may hold values from -6 to 6
- values: bfloat16 [8192, 1024], P(('groups', 'events'), 'heads'), parts along dimension 0, may hold values from -6 to 6
- gain: float32 [1024], P('heads'), may hold values from 0.1 to 1.9
- w_out: bfloat16 [1024, 1024], P('heads'), may hold values from -0.1875 to 0.1875
Outputs:
- scored: bfloat16 [256, 1024], P(('groups', 'events')), parts along dimension 0
There are 2 independent parts, one for each index of `groups`. A program takes and returns all parts, laid end to end along the dimension named above; an argument that names none is the same for every part. Nothing has to cross between parts.
Inputs may be any that keep to these rules, and one draw needn't show every extreme that they name: `event_count`: each cache shard's filled slots come first; some shard is full and some holds 128. `event_user`: Users' events are consecutive and in increasing user order over the whole cache; every user has 1 to 2047 events, and some user has exactly 2047. `cand_user`: every candidate belongs to a user that has at least one filled slot somewhere in the cache.
All inputs are finite; a program needn't handle non-finite values.
Results may differ from a plain program's by a relative error of at most 0.0075.
Values may be sent and summed in bfloat16 or wider, within the bound.
No kernel may reach another device: no remote copies, remote signals or barrier semaphores. Data moves between devices by JAX's collectives and lax.ppermute only.
A program may use at most 64 MiB of HBM per device.

v0:
```python
import math
import jax
import jax.numpy as jnp
from jax import lax
from jax.sharding import PartitionSpec as P

DH = 128
HD = 1024
epsilon = 1e-05


def shards(inputs, cand_user, event_user, event_count, w_qu, keys, values, gain, w_out):
    row_count = inputs.shape[0]
    feat_width = inputs.shape[1]
    local_width = w_qu.shape[2]
    heads_here = local_width // DH
    slot_total = keys.shape[0]
    score_scale = 1.0 / math.sqrt(DH)
    packed_weight = w_qu.reshape(feat_width, 2 * local_width)
    query_weight = packed_weight[:, :local_width]
    gate_weight = packed_weight[:, local_width:]
    gate_values = jax.nn.silu(
        jnp.dot(inputs, gate_weight, preferred_element_type=jnp.float32)
    ).astype(jnp.bfloat16)
    gathered_rows = lax.all_gather(inputs, "events", axis=0, tiled=True)
    queries = jax.nn.silu(
        jnp.dot(gathered_rows, query_weight, preferred_element_type=jnp.float32)
    ).astype(jnp.bfloat16)
    slot_index = jnp.arange(slot_total, dtype=jnp.int32)
    slot_valid = slot_index < event_count[0]
    key_heads = keys.reshape(slot_total, heads_here, DH)
    value_heads = values.reshape(slot_total, heads_here, DH)

    def attend_rows(query_rows, row_users):
        rows_here = query_rows.shape[0]
        query_block = query_rows.reshape(rows_here, heads_here, DH)
        user_match = ((row_users[:, None] == event_user[None, :]) & slot_valid[None, :]).astype(
            jnp.float32
        )
        scores = (
            jnp.einsum("chd,ehd->hce", query_block, key_heads, preferred_element_type=jnp.float32)
            * score_scale
        )
        attn_weights = (jax.nn.silu(scores) * user_match[None]).astype(jnp.bfloat16)
        partial_out = jnp.einsum(
            "hce,ehd->chd", attn_weights, value_heads, preferred_element_type=jnp.float32
        )
        return partial_out.reshape(rows_here, local_width)

    block_rows = math.gcd(row_count * lax.axis_size("events"), 512)
    block_count = row_count * lax.axis_size("events") // block_rows

    def compute_block(which_block):
        block_start = which_block * block_rows
        query_rows = lax.dynamic_slice_in_dim(queries, block_start, block_rows, 0)
        block_users = lax.dynamic_slice_in_dim(cand_user, block_start, block_rows, 0)
        return attend_rows(query_rows, block_users)

    stacked = lax.map(compute_block, jnp.arange(block_count, dtype=jnp.int32))
    attended = lax.psum_scatter(
        stacked.reshape(row_count * lax.axis_size("events"), local_width),
        "events",
        scatter_dimension=0,
        tiled=True,
    )
    first_moment = jnp.sum(attended, axis=1)
    second_moment = jnp.sum(attended * attended, axis=1)
    total_first, total_second = lax.psum((first_moment, second_moment), "heads")
    average = total_first / HD
    variance = total_second / HD - average * average
    normed = (attended - average[:, None]) * lax.rsqrt(variance + epsilon)[:, None] * gain
    gated = (normed * gate_values.astype(jnp.float32)).astype(jnp.bfloat16)
    projected = jnp.dot(gated, w_out, preferred_element_type=jnp.float32)
    summed_heads = lax.psum(projected, "heads")
    return (inputs.astype(jnp.float32) + summed_heads).astype(jnp.bfloat16)


def solution(mesh):
    placed = (
        P(("groups", "events"), None),
        P("groups"),
        P(("groups", "events")),
        P(("groups", "events")),
        P(None, None, "heads"),
        P(("groups", "events"), "heads"),
        P(("groups", "events"), "heads"),
        P("heads"),
        P("heads", None),
    )
    return jax.shard_map(
        shards, mesh=mesh, in_specs=placed, out_specs=P(("groups", "events"), None), check_vma=False
    )
```

profile of v0, /device:TPU:0, one launch (start us, length us, event | category | flops | bytes accessed | tf_op | source)
XLA Modules:
  0.0 143.9 jit_solution(11439747766623471906)
XLA Ops:
  6.5 0.0 copy-start
  6.5 0.0 reduce-scatter.2.cloned.1.call-start
  7.3 32.8 %all_gather.3 = bf16[128,1024]{1,0:T(8,128)(2,1)S(1)} all-gather(bf16[16,1024]{1,0:T(8,128)(2,1)} %param.9), channel_id=1, replica_groups=mesh['groups'=2,'events'=8,'heads'=2] {'events'}, dimensions={0}, use_global_device_ids=true | all-gather | bytes 294912 | tf_op jit(solution)/shard_map/all_gather | solution.py:25
  40.1 2.0 %copy.14 = bf16[512,512]{0,1:T(8,128)(2,1)} copy(bf16[512,512]{1,0:T(8,128)(2,1)} %param.15) | data formatting | bytes 1048576 | tf_op jit(solution)/shard_map/reshape | solution.py:32
  42.1 2.2 %copy.17 = bf16[128,8,2,512]{3,1,2,0:T(8,128)(2,1)S(1)} copy(bf16[128,8,2,512]{3,2,1,0:T(2,128)(2,1)} %bitcast.29) | data formatting | bytes 4194304
  44.3 0.0 copy-start.2
  44.3 0.0 copy-start.4
  44.3 1.0 fusion.14
  45.3 0.0 copy-done.2
  45.3 0.0 copy-done.4
  45.3 0.1 and_convert_fusion
  45.4 0.0 copy-start.1
  45.4 0.0 copy-start.3
  45.4 2.6 %fusion.4 = f32[4,128,128]{1,2,0:T(8,128)} fusion(bf16[512,4,128]{0,2,1:T(8,128)(2,1)} %bitcast.30, f32[128,512]{1,0:T(8,128)S(1)} %and_convert_fusion, bf16[16,4,8,128]{3,2,1,0:T(8,128)(2,1)} %fusion.14, bf16[512,512]{1,0:T(8,128)(2,1)} %param.14), kind=kOutput, calls=%fused_computation.6 | convolution fusion | flops 136052736 | bytes 1703936 | tf_op jit(solution)/shard_map/while/body/eval_jaxpr/hce,ehd->chd/dot_general | solution.py:45
  48.1 1.8 %copy.13 = f32[128,512]{1,0:T(8,128)} copy(f32[128,512]{0,1:T(8,128)} %bitcast.31) | data formatting | bytes 524288 | tf_op jit(solution)/shard_map/reshape | solution.py:61
  49.9 0.0 reduce-scatter.2.cloned.1.call-update
  49.9 0.0 all-reduce.3.cloned.1.call-start
  49.9 63.5 %reduce-scatter.2.cloned.1.call-done = f32[16,512]{1,0:T(8,128)} async-done(((f32[128,512]{1,0:T(8,128)}), f32[16,512]{1,0:T(8,128)}) %reduce-scatter.2.cloned.1.call-update) | async-done | bytes 32784 | tf_op jit(solution)/shard_map/reduce_scatter | solution.py:60
  113.5 0.9 fusion.38
  114.3 2.5 %all-reduce = (f32[16]{0:T(128)S(1)}, f32[16]{0:T(128)S(1)}) all-reduce(f32[16]{0:T(128)S(1)} %get-tuple-element.20, f32[16]{0:T(128)S(1)} %get-tuple-element.19), channel_id=1, replica_groups=mesh['groups'=2,'events'=8,'heads'=2] {'heads'}, use_global_device_ids=true, to_apply=%region_4.5 | all-reduce | flops 32 | bytes 256 | tf_op jit(solution)/shard_map/psum | solution.py:68
  116.8 0.0 copy-done
  116.8 0.0 copy-done.1
  116.8 0.0 copy-done.3
  116.8 1.9 %fusion.26 = f32[16,1024]{1,0:T(8,128)} fusion(bf16[512,1024]{1,0:T(8,128)(2,1)S(1)} %copy-done, bf16[16,1024]{1,0:T(8,128)(2,1)S(1)} %copy-done.1, bf16[1024,1024]{1,0:T(8,128)(2,1)S(1)} %bitcast.28, f32[16,512]{1,0:T(8,128)} %reduce-scatter.2.cloned.1.call-done, f32[512]{0:T(512)S(1)} %copy-done.3, f32[16]{0:T(128)S(1)} %get-tuple-element.32, ...), kind=kOutput, calls=%fused_computation.20 | convolution fusion | flops 33644544 | bytes 2231296 | tf_op jit(solution)/shard_map/dot_general | solution.py:73
  118.7 0.0 all-reduce.3.cloned.1.call-update
  118.7 16.9 %all-reduce.3.cloned.1.call-done = f32[16,1024]{1,0:T(8,128)} async-done(((f32[16,1024]{1,0:T(8,128)}), f32[16,1024]{1,0:T(8,128)}) %all-reduce.3.cloned.1.call-update) | async-done | bytes 65552 | tf_op jit(solution)/shard_map/psum | solution.py:74
  135.6 1.5 %add_convert_fusion = bf16[16,1024]{1,0:T(8,128)(2,1)} fusion(f32[16,1024]{1,0:T(8,128)} %all-reduce.3.cloned.1.call-done, bf16[16,1024]{1,0:T(8,128)(2,1)S(1)} %copy-done.1), kind=kLoop, calls=%fused_computation.17 | loop fusion | flops 49152 | bytes 131072 | tf_op jit(solution)/shard_map/convert_element_type | solution.py:75
  (2 shorter events, 0.0 us)
Async XLA Ops:
  6.5 110.3 %copy-start = (bf16[512,1024]{1,0:T(8,128)(2,1)S(1)}, bf16[512,1024]{1,0:T(8,128)(2,1)}, u32[]{:S(2)}) copy-start(bf16[512,1024]{1,0:T(8,128)(2,1)} %param.17) | copy-start | bytes 3145732
  6.5 106.9 %reduce-scatter.2.cloned.1.call-start = ((), (), s32[]{:S(2)}) async-start(), calls=%async_computation.1 | async-start | bytes 294912 | tf_op jit(solution)/shard_map/reduce_scatter | solution.py:60
  44.3 1.0 copy-start.2
  44.3 1.0 copy-start.4
  45.4 71.4 %copy-start.1 = (bf16[16,1024]{1,0:T(8,128)(2,1)S(1)}, bf16[16,1024]{1,0:T(8,128)(2,1)}, u32[]{:S(2)}) copy-start(bf16[16,1024]{1,0:T(8,128)(2,1)} %param.9) | copy-start | bytes 98308
  45.4 71.4 %copy-start.3 = (f32[512]{0:T(512)S(1)}, f32[512]{0:T(512)}, u32[]{:S(2)}) copy-start(f32[512]{0:T(512)} %param.16) | copy-start | bytes 6148
  49.9 85.7 %all-reduce.3.cloned.1.call-start = ((), (), s32[]{:S(2)}) async-start(), calls=%async_computation.2 | async-start | bytes 131072 | tf_op jit(solution)/shard_map/psum | solution.py:74
Sparse Core Ops, SparseCore 0:
  50.0 63.4 reduce-scatter.1
  118.8 16.7 all-reduce.2
where the time goes:
time: 144 us
  waiting for transfers between devices  80.5 us (56%)
  blocking collectives  35.2 us (24%)
  between operations  14.2 us (10%)
  local copies, waits for them, and re-layouts  6 us (4%)
  matrix products  5.52 us (4%)
  other arithmetic  2.45 us (2%)
    reduce_scatter x1, waiting for transfers between devices, shards(): lax.psum_scatter(stacked.reshape(row_count * lax.axis_size('events'), loc...  63.5 us
    all_gather x1, blocking collectives, shards(): gathered_rows = lax.all_gather(inputs, 'events', axis=0, tiled=True)  32.8 us
    psum x1, waiting for transfers between devices, shards(): summed_heads = lax.psum(projected, 'heads')  16.9 us
  transfers between devices with their start and end apart: 2, of which 2 were waited for; matrix products, arithmetic and copies ran while one was open for 0% of the time, Pallas kernels for 0%

commit v1 on v0

--- a/solution.py
+++ b/solution.py
@@ -71,7 +71,7 @@
     normed = (attended - average[:, None]) * lax.rsqrt(variance + epsilon)[:, None] * gain
     gated = (normed * gate_values.astype(jnp.float32)).astype(jnp.bfloat16)
     projected = jnp.dot(gated, w_out, preferred_element_type=jnp.float32)
-    summed_heads = lax.psum(projected, "heads")
+    summed_heads = jnp.sum(lax.all_gather(projected, "heads"), axis=0)
     return (inputs.astype(jnp.float32) + summed_heads).astype(jnp.bfloat16)
 
 

time: 144 us -> 128 us (0.89)
  waiting for transfers between devices: 80.5 us -> 63.6 us
  blocking collectives: 35.2 us -> 37.1 us
    psum x1 -> x0, waiting for transfers between devices: 16.9 us -> none  [shards(): summed_heads = lax.psum(projected, 'heads')]
    all_gather x0 -> x1, blocking collectives: none -> 1.9 us  [shards(): summed_heads = jnp.sum(lax.all_gather(projected, 'heads'), axis=0)]
  transfers between devices with their start and end apart: 2 -> 1, of which waited for: 2 -> 1; matrix products, arithmetic and copies ran while one was open for 0% -> 0% of each run, Pallas kernels for 0% -> 0%
where the time goes in v1:
time: 128 us; the launch traced here: 127 us
  waiting for transfers between devices  63.6 us (50%)
  blocking collectives  37.1 us (29%)
  between operations  14.2 us (11%)
  local copies, waits for them, and re-layouts  6 us (5%)
  matrix products  4.89 us (4%)
  other arithmetic  1.63 us (1%)
    reduce_scatter x1, waiting for transfers between devices, shards(): lax.psum_scatter(stacked.reshape(row_count * lax.axis_size('events'), loc...  63.6 us
    all_gather x1, blocking collectives, shards(): gathered_rows = lax.all_gather(inputs, 'events', axis=0, tiled=True)  32.8 us
    dot_general x1, matrix products, attend_rows(): jnp.einsum('hce,ehd->chd', attn_weights, value_heads, preferred_element_t...  2.65 us
  transfers between devices with their start and end apart: 1, of which 1 were waited for; matrix products, arithmetic and copies ran while one was open for 0% of the time, Pallas kernels for 0%

profile of v1, /device:TPU:0, one launch (start us, length us, event | category | flops | bytes accessed | tf_op | source)
XLA Modules:
  0.0 127.4 jit_solution(3170197751630035930)
XLA Ops:
  6.5 0.0 copy-start
  6.5 0.0 reduce-scatter.2.cloned.1.call-start
  7.3 32.8 %all_gather.9 = bf16[128,1024]{1,0:T(8,128)(2,1)S(1)} all-gather(bf16[16,1024]{1,0:T(8,128)(2,1)} %param.9), channel_id=1, replica_groups=mesh['groups'=2,'events'=8,'heads'=2] {'events'}, dimensions={0}, use_global_device_ids=true | all-gather | bytes 294912 | tf_op jit(solution)/shard_map/all_gather | solution.py:25
  40.1 2.0 %copy.14 = bf16[512,512]{0,1:T(8,128)(2,1)} copy(bf16[512,512]{1,0:T(8,128)(2,1)} %param.15) | data formatting | bytes 1048576 | tf_op jit(solution)/shard_map/reshape | solution.py:32
  42.1 2.2 %copy.17 = bf16[128,8,2,512]{3,1,2,0:T(8,128)(2,1)S(1)} copy(bf16[128,8,2,512]{3,2,1,0:T(2,128)(2,1)} %bitcast.30) | data formatting | bytes 4194304
  44.3 0.0 copy-start.2
  44.3 0.0 copy-start.4
  44.3 1.0 fusion.14
  45.3 0.0 copy-done.2
  45.3 0.0 copy-done.4
  45.3 0.1 and_convert_fusion
  45.4 0.0 copy-start.1
  45.4 0.0 copy-start.3
  45.4 2.6 %fusion.4 = f32[4,128,128]{1,2,0:T(8,128)} fusion(bf16[512,4,128]{0,2,1:T(8,128)(2,1)} %bitcast.32, f32[128,512]{1,0:T(8,128)S(1)} %and_convert_fusion, bf16[16,4,8,128]{3,2,1,0:T(8,128)(2,1)} %fusion.14, bf16[512,512]{1,0:T(8,128)(2,1)} %param.14), kind=kOutput, calls=%fused_computation.6 | convolution fusion | flops 136052736 | bytes 1703936 | tf_op jit(solution)/shard_map/while/body/eval_jaxpr/hce,ehd->chd/dot_general | solution.py:45
  48.1 1.8 %copy.13 = f32[128,512]{1,0:T(8,128)} copy(f32[128,512]{0,1:T(8,128)} %bitcast.33) | data formatting | bytes 524288 | tf_op jit(solution)/shard_map/reshape | solution.py:61
  49.9 0.0 reduce-scatter.2.cloned.1.call-update
  49.9 63.6 %reduce-scatter.2.cloned.1.call-done = f32[16,512]{1,0:T(8,128)} async-done(((f32[128,512]{1,0:T(8,128)}), f32[16,512]{1,0:T(8,128)}) %reduce-scatter.2.cloned.1.call-update) | async-done | bytes 32784 | tf_op jit(solution)/shard_map/reduce_scatter | solution.py:60
  113.5 0.9 fusion.38
  114.3 2.5 %all-reduce = (f32[16]{0:T(128)S(1)}, f32[16]{0:T(128)S(1)}) all-reduce(f32[16]{0:T(128)S(1)} %get-tuple-element.20, f32[16]{0:T(128)S(1)} %get-tuple-element.19), channel_id=1, replica_groups=mesh['groups'=2,'events'=8,'heads'=2] {'heads'}, use_global_device_ids=true, to_apply=%region_4.5 | all-reduce | flops 32 | bytes 256 | tf_op jit(solution)/shard_map/psum | solution.py:68
  116.8 0.0 copy-done
  116.8 0.0 copy-done.1
  116.8 0.0 copy-done.3
  116.8 1.2 fusion.26
  118.1 1.9 %all-gather = f32[32,1024]{1,0:T(8,128)S(1)} all-gather(f32[16,1024]{1,0:T(8,128)S(1)} %fusion.26), channel_id=2, replica_groups=mesh['groups'=2,'events'=8,'heads'=2] {'heads'}, dimensions={0}, use_global_device_ids=true | all-gather | bytes 196608 | tf_op jit(solution)/shard_map/all_gather | solution.py:74
  120.0 0.6 add_convert_fusion
  (3 shorter events, 0.0 us)
Async XLA Ops:
  6.5 110.3 %copy-start = (bf16[512,1024]{1,0:T(8,128)(2,1)S(1)}, bf16[512,1024]{1,0:T(8,128)(2,1)}, u32[]{:S(2)}) copy-start(bf16[512,1024]{1,0:T(8,128)(2,1)} %param.17) | copy-start | bytes 3145732
  6.5 106.9 %reduce-scatter.2.cloned.1.call-start = ((), (), s32[]{:S(2)}) async-start(), calls=%async_computation.1 | async-start | bytes 294912 | tf_op jit(solution)/shard_map/reduce_scatter | solution.py:60
  44.3 1.0 copy-start.2
  44.3 1.0 copy-start.4
  45.4 71.4 %copy-start.1 = (bf16[16,1024]{1,0:T(8,128)(2,1)S(1)}, bf16[16,1024]{1,0:T(8,128)(2,1)}, u32[]{:S(2)}) copy-start(bf16[16,1024]{1,0:T(8,128)(2,1)} %param.9) | copy-start | bytes 98308
  45.4 71.4 %copy-start.3 = (f32[512]{0:T(512)S(1)}, f32[512]{0:T(512)}, u32[]{:S(2)}) copy-start(f32[512]{0:T(512)} %param.16) | copy-start | bytes 6148
Sparse Core Ops, SparseCore 0:
  50.0 63.4 reduce-scatter.1
